TPU v7x, 32 devices: a whole 2x2x4 slice. The times are simulated.
32 devices in a mesh: row: 4 (over y, x), col: 8 (over z, core).
Axes of the slice: x: 2, y: 2, z: 4, core: 2. Of those that a mesh axis runs over, the one named last changes fastest.
Arguments:
- density: float32 [2048, 2048], P('row', 'col'), as said below
- pattern: int32 [16, 16], replicated, may hold values from 0 to 1, as said below
Outputs:
- purified: float32 [2048, 2048], P('row', 'col')
Inputs may be any that keep to these rules, and one draw needn't show every extreme that they name: density is symmetric and zero outside the blocks that pattern allows. pattern is symmetric with ones on its diagonal, and every block row holds exactly 7 ones.
All inputs are finite; a program needn't handle non-finite values.
Results may differ from a plain program's by a relative error of at most 0.0061.
Values may be sent and summed in bfloat16 or wider, within the bound.
No kernel may reach another device: no remote copies, remote signals or barrier semaphores. Data moves between devices by JAX's collectives and lax.ppermute only.
A program may use at most 64 MiB of HBM per device.

v0:
```python
import jax
import jax.numpy as jnp
from jax import lax
from jax.sharding import PartitionSpec as P

BS = 128
STEPS = 2


def allowed_blocks(pattern):
    count = pattern.shape[0]
    index = lax.iota(jnp.int32, count)
    eye = (index[:, None] == index[None, :]).astype(jnp.int32)
    return jnp.maximum(jnp.maximum(pattern, pattern.T), eye)


def apply_mask(values, blocks):
    row_blocks, col_blocks = blocks.shape
    shaped = values.reshape(row_blocks, BS, col_blocks, BS) * blocks[:, None, :, None]
    return shaped.reshape(row_blocks * BS, col_blocks * BS)


def on_device(density, pattern):
    rows, cols = density.shape
    row_blocks = rows // BS
    col_blocks = cols // BS
    allowed = allowed_blocks(pattern)
    first_row = lax.axis_index("row") * row_blocks
    first_col = lax.axis_index("col") * col_blocks
    blocks = lax.dynamic_slice(allowed, (first_row, first_col), (row_blocks, col_blocks)).astype(
        jnp.float32
    )
    current = apply_mask(density, blocks)
    for step in range(STEPS):
        xb = current.astype(jnp.bfloat16)
        x_panel = lax.all_gather(xb, "row", axis=0, tiled=True)
        square = jnp.dot(
            lax.all_gather(xb, "col", axis=1, tiled=True),
            x_panel,
            preferred_element_type=jnp.float32,
        )
        square = apply_mask(square, blocks)
        qb = square.astype(jnp.bfloat16)
        q_panel = lax.all_gather(qb, "row", axis=0, tiled=True)
        total = jnp.dot(
            lax.all_gather(qb, "col", axis=1, tiled=True),
            x_panel,
            preferred_element_type=jnp.float32,
        )
        jordan = total + jnp.dot(
            lax.all_gather(xb, "col", axis=1, tiled=True),
            q_panel,
            preferred_element_type=jnp.float32,
        )
        current = apply_mask(3.0 * square - jordan, blocks)
    return current


def solution(mesh):
    placed = (P("row", "col"), P())
    return jax.shard_map(
        on_device, mesh=mesh, in_specs=placed, out_specs=P("row", "col"), check_vma=False
    )
```

profile of v0, /device:TPU:0, one launch (start us, length us, event | category | flops | bytes accessed | tf_op | source)
XLA Modules:
  0.0 265.3 jit_solution(4661226299853887989)
XLA Ops:
  6.5 0.0 all-gather.11.cloned.1.call-start
  6.5 0.8 copy.3
  7.3 0.8 fusion.7
  8.1 0.2 mul.53
  8.3 1.8 fusion.5
  10.1 0.0 all-gather.11.cloned.1.call-update
  10.1 0.0 all-gather.9.cloned.1.call-start
  10.2 0.7 all-gather.9.cloned.1.call-update
  10.9 0.0 all-gather.13.cloned.1.call-start
  10.9 28.7 %all-gather.11.cloned.1.call-done = bf16[2048,256]{1,0:T(8,128)(2,1)} async-done(((bf16[512,256]{1,0:T(8,128)(2,1)}), bf16[2048,256]{1,0:T(8,128)(2,1)}) %all-gather.11.cloned.1.call-update) | async-done | bytes 1048592 | tf_op jit(solution)/shard_map/all_gather | solution.py:36
  39.6 32.5 %all-gather.9.cloned.1.call-done = bf16[512,2048]{1,0:T(8,128)(2,1)} async-done(((bf16[512,256]{1,0:T(8,128)(2,1)}), bf16[512,2048]{1,0:T(8,128)(2,1)}) %all-gather.9.cloned.1.call-update) | async-done | bytes 2097168 | tf_op jit(solution)/shard_map/all_gather | solution.py:38
  72.0 3.3 %fusion.8 = (bf16[512,256]{1,0:T(8,128)(2,1)}, f32[512,256]{1,0:T(8,128)S(1)}) fusion(f32[64,8,2,128]{3,2,1,0:T(2,128)S(1)} %bitcast.24, bf16[512,2048]{1,0:T(8,128)(2,1)} %all-gather.9.cloned.1.call-done, bf16[2048,256]{1,0:T(8,128)(2,1)} %all-gather.11.cloned.1.call-done), kind=kOutput, calls=%fused_computation.15 | convolution fusion | flops 537133056 | bytes 4456448 | tf_op jit(solution)/shard_map/dot_general | solution.py:37
  75.3 0.0 all-gather.13.cloned.1.call-update
  75.3 0.0 copy-start.1
  75.3 0.0 all-gather.15.cloned.1.call-start
  75.4 0.5 all-gather.15.cloned.1.call-update
  75.9 0.0 all-gather.19.cloned.1.call-start
  76.0 29.4 %all-gather.13.cloned.1.call-done = bf16[512,2048]{1,0:T(8,128)(2,1)} async-done(((bf16[512,256]{1,0:T(8,128)(2,1)}), bf16[512,2048]{1,0:T(8,128)(2,1)}) %all-gather.13.cloned.1.call-update) | async-done | bytes 2097168 | tf_op jit(solution)/shard_map/all_gather | solution.py:46
  105.4 3.4 %fusion.10 = f32[512,256]{1,0:T(8,128)} fusion(bf16[512,2048]{1,0:T(8,128)(2,1)} %all-gather.13.cloned.1.call-done, bf16[2048,256]{1,0:T(8,128)(2,1)} %all-gather.11.cloned.1.call-done), kind=kOutput, calls=%fused_computation.17 | convolution fusion | flops 536870912 | bytes 3670016 | tf_op jit(solution)/shard_map/dot_general | solution.py:45
  108.8 24.1 %all-gather.15.cloned.1.call-done = bf16[2048,256]{1,0:T(8,128)(2,1)} async-done(((bf16[512,256]{1,0:T(8,128)(2,1)}), bf16[2048,256]{1,0:T(8,128)(2,1)}) %all-gather.15.cloned.1.call-update) | async-done | bytes 1048592 | tf_op jit(solution)/shard_map/all_gather | solution.py:44
  132.8 0.0 copy-done.1
  132.8 2.8 %fusion.4 = bf16[512,256]{1,0:T(8,128)(2,1)} fusion(f32[512,256]{1,0:T(8,128)} %fusion.10, bf16[512,2048]{1,0:T(8,128)(2,1)S(1)} %copy-done.1, bf16[2048,256]{1,0:T(8,128)(2,1)} %all-gather.15.cloned.1.call-done, f32[512,256]{1,0:T(8,128)S(1)} %get-tuple-element.6, f32[64,8,2,128]{3,2,1,0:T(2,128)S(1)} %bitcast.25), kind=kOutput, calls=%fused_computation.8 | convolution fusion | flops 537526272 | bytes 4980736 | tf_op jit(solution)/shard_map/dot_general | solution.py:50
  135.6 0.0 all-gather.19.cloned.1.call-update
  135.6 0.0 all-gather.17.cloned.1.call-start
  135.7 0.5 all-gather.17.cloned.1.call-update
  136.2 0.0 all-gather.21.cloned.1.call-start
  136.2 26.1 %all-gather.19.cloned.1.call-done = bf16[2048,256]{1,0:T(8,128)(2,1)} async-done(((bf16[512,256]{1,0:T(8,128)(2,1)}), bf16[2048,256]{1,0:T(8,128)(2,1)}) %all-gather.19.cloned.1.call-update) | async-done | bytes 1048592 | tf_op jit(solution)/shard_map/all_gather | solution.py:36
  162.4 32.3 %all-gather.17.cloned.1.call-done = bf16[512,2048]{1,0:T(8,128)(2,1)} async-done(((bf16[512,256]{1,0:T(8,128)(2,1)}), bf16[512,2048]{1,0:T(8,128)(2,1)}) %all-gather.17.cloned.1.call-update) | async-done | bytes 2097168 | tf_op jit(solution)/shard_map/all_gather | solution.py:38
  194.7 3.3 %fusion.9 = (bf16[512,256]{1,0:T(8,128)(2,1)}, f32[512,256]{1,0:T(8,128)S(1)}) fusion(f32[64,8,2,128]{3,2,1,0:T(2,128)S(1)} %bitcast.26, bf16[512,2048]{1,0:T(8,128)(2,1)} %all-gather.17.cloned.1.call-done, bf16[2048,256]{1,0:T(8,128)(2,1)} %all-gather.19.cloned.1.call-done), kind=kOutput, calls=%fused_computation.16 | convolution fusion | flops 537133056 | bytes 4456448 | tf_op jit(solution)/shard_map/dot_general | solution.py:37
  198.0 0.0 all-gather.21.cloned.1.call-update
  198.0 0.0 copy-start
  198.0 0.0 all-gather.23.cloned.1.call-start
  198.1 0.7 all-gather.23.cloned.1.call-update
  198.8 29.3 %all-gather.21.cloned.1.call-done = bf16[512,2048]{1,0:T(8,128)(2,1)} async-done(((bf16[512,256]{1,0:T(8,128)(2,1)}), bf16[512,2048]{1,0:T(8,128)(2,1)}) %all-gather.21.cloned.1.call-update) | async-done | bytes 2097168 | tf_op jit(solution)/shard_map/all_gather | solution.py:46
  228.1 3.4 %fusion.11 = f32[512,256]{1,0:T(8,128)} fusion(bf16[512,2048]{1,0:T(8,128)(2,1)} %all-gather.21.cloned.1.call-done, bf16[2048,256]{1,0:T(8,128)(2,1)} %all-gather.19.cloned.1.call-done), kind=kOutput, calls=%fused_computation.18 | convolution fusion | flops 536870912 | bytes 3670016 | tf_op jit(solution)/shard_map/dot_general | solution.py:45
  231.4 24.2 %all-gather.23.cloned.1.call-done = bf16[2048,256]{1,0:T(8,128)(2,1)} async-done(((bf16[512,256]{1,0:T(8,128)(2,1)}), bf16[2048,256]{1,0:T(8,128)(2,1)}) %all-gather.23.cloned.1.call-update) | async-done | bytes 1048592 | tf_op jit(solution)/shard_map/all_gather | solution.py:44
  255.6 0.0 copy-done
  255.6 2.9 %fusion.3 = f32[512,256]{1,0:T(8,128)} fusion(f32[512,256]{1,0:T(8,128)} %fusion.11, bf16[512,2048]{1,0:T(8,128)(2,1)S(1)} %copy-done, bf16[2048,256]{1,0:T(8,128)(2,1)} %all-gather.23.cloned.1.call-done, f32[512,256]{1,0:T(8,128)S(1)} %get-tuple-element.8, f32[64,8,2,128]{3,2,1,0:T(2,128)S(1)} %bitcast.27), kind=kOutput, calls=%fused_computation.7 | convolution fusion | flops 537395200 | bytes 5242880 | tf_op jit(solution)/shard_map/dot_general | solution.py:50
Async XLA Ops:
  6.5 33.0 %all-gather.11.cloned.1.call-start = ((), (), s32[]{:S(2)}) async-start(), calls=%async_computation.1 | async-start | bytes 1310720 | tf_op jit(solution)/shard_map/all_gather | solution.py:36
  10.1 61.9 %all-gather.9.cloned.1.call-start = ((), (), s32[]{:S(2)}) async-start(), calls=%async_computation | async-start | bytes 2359296 | tf_op jit(solution)/shard_map/all_gather | solution.py:38
  10.9 94.5 %all-gather.13.cloned.1.call-start = ((), (), s32[]{:S(2)}) async-start(), calls=%async_computation.2 | async-start | bytes 2359296 | tf_op jit(solution)/shard_map/all_gather | solution.py:46
  75.3 57.5 %copy-start.1 = (bf16[512,2048]{1,0:T(8,128)(2,1)S(1)}, bf16[512,2048]{1,0:T(8,128)(2,1)}, u32[]{:S(2)}) copy-start(bf16[512,2048]{1,0:T(8,128)(2,1)} %all-gather.9.cloned.1.call-done) | copy-start | bytes 6291460
  75.3 57.5 %all-gather.15.cloned.1.call-start = ((), (), s32[]{:S(2)}) async-start(), calls=%async_computation.3 | async-start | bytes 1310720 | tf_op jit(solution)/shard_map/all_gather | solution.py:44
  75.9 86.5 %all-gather.19.cloned.1.call-start = ((), (), s32[]{:S(2)}) async-start(), calls=%async_computation.5 | async-start | bytes 1310720 | tf_op jit(solution)/shard_map/all_gather | solution.py:36
  135.6 59.1 %all-gather.17.cloned.1.call-start = ((), (), s32[]{:S(2)}) async-start(), calls=%async_computation.4 | async-start | bytes 2359296 | tf_op jit(solution)/shard_map/all_gather | solution.py:38
  136.2 91.9 %all-gather.21.cloned.1.call-start = ((), (), s32[]{:S(2)}) async-start(), calls=%async_computation.6 | async-start | bytes 2359296 | tf_op jit(solution)/shard_map/all_gather | solution.py:46
  198.0 57.6 %copy-start = (bf16[512,2048]{1,0:T(8,128)(2,1)S(1)}, bf16[512,2048]{1,0:T(8,128)(2,1)}, u32[]{:S(2)}) copy-start(bf16[512,2048]{1,0:T(8,128)(2,1)} %all-gather.17.cloned.1.call-done) | copy-start | bytes 6291460
  198.0 57.6 %all-gather.23.cloned.1.call-start = ((), (), s32[]{:S(2)}) async-start(), calls=%async_computation.7 | async-start | bytes 1310720 | tf_op jit(solution)/shard_map/all_gather | solution.py:44
Sparse Core Ops, SparseCore 0:
  10.2 29.3 all-gather.10
  41.2 30.8 all-gather.8
  75.5 29.8 all-gather.12
  107.1 25.6 all-gather.14
  135.7 26.6 all-gather.18
  163.8 30.8 all-gather.16
  198.1 29.8 all-gather.20
  229.9 25.6 all-gather.22
where the time goes:
time: 266 us; the launch traced here: 265 us
  waiting for transfers between devices  229 us (86%)
  matrix products  18.9 us (7%)
  between operations  13.5 us (5%)
    all_gather x2, waiting for transfers between devices, on_device(): lax.all_gather(xb, 'col', axis=1, tiled=True)  64.8 us
    all_gather x2, waiting for transfers between devices, on_device(): lax.all_gather(qb, 'col', axis=1, tiled=True)  58.7 us
    all_gather x2, waiting for transfers between devices, on_device(): x_panel = lax.all_gather(xb, 'row', axis=0, tiled=True)  54.8 us
    all_gather x2, waiting for transfers between devices, on_device(): q_panel = lax.all_gather(qb, 'row', axis=0, tiled=True)  48.3 us
    dot_general x2, matrix products, on_device(): jnp.dot(lax.all_gather(qb, 'col', axis=1, tiled=True), x_panel, preferred...  6.72 us
    dot_general x2, matrix products, on_device(): jnp.dot(lax.all_gather(xb, 'col', axis=1, tiled=True), x_panel, preferred...  6.54 us
    dot_general x2, matrix products, on_device(): jnp.dot(lax.all_gather(xb, 'col', axis=1, tiled=True), q_panel, preferred...  5.63 us
  transfers between devices with their start and end apart: 8, of which 8 were waited for; matrix products, arithmetic and copies ran while one was open for 3% of the time, Pallas kernels for 0%

commit v1 on v0

--- a/solution.py
+++ b/solution.py
@@ -5,6 +5,27 @@
 
 BS = 128
 STEPS = 2
+
+
+def collect(x, axis, dim):
+    peers, index, span = (lax.axis_size(axis), lax.axis_index(axis), x.shape[dim])
+    right = [(i, (i + 1) % peers) for i in range(peers)]
+    left = [(i, (i - 1) % peers) for i in range(peers)]
+    out = jnp.zeros((*x.shape[:dim], peers * span, *x.shape[dim + 1 :]), x.dtype)
+    out = lax.dynamic_update_slice_in_dim(out, x, index * span, axis=dim)
+    from_left = from_right = x
+    halfway = peers // 2
+    for hop in range(1, halfway + 1):
+        from_left = lax.ppermute(from_left, axis, right)
+        out = lax.dynamic_update_slice_in_dim(
+            out, from_left, (index - hop) % peers * span, axis=dim
+        )
+        if hop < peers - halfway:
+            from_right = lax.ppermute(from_right, axis, left)
+            out = lax.dynamic_update_slice_in_dim(
+                out, from_right, (index + hop) % peers * span, axis=dim
+            )
+    return out
 
 
 def allowed_blocks(pattern):
@@ -41,7 +62,7 @@
         )
         square = apply_mask(square, blocks)
         qb = square.astype(jnp.bfloat16)
-        q_panel = lax.all_gather(qb, "row", axis=0, tiled=True)
+        q_panel = collect(qb, "row", 0)
         total = jnp.dot(
             lax.all_gather(qb, "col", axis=1, tiled=True),
             x_panel,

time: 266 us -> 218 us (0.82)
  waiting for transfers between devices: 229 us -> 168 us
  local copies, waits for them, and re-layouts: 0.98 us -> 8.32 us
  starting transfers between devices: 0.28 us -> 6.76 us
    all_gather x2 -> x0, waiting for transfers between devices: 48.3 us -> none  [on_device(): q_panel = lax.all_gather(qb, 'row', axis=0, tiled=True)]
    all_gather x2, waiting for transfers between devices: 58.7 us -> 15.9 us  [on_device(): lax.all_gather(qb, 'col', axis=1, tiled=True)]
    ppermute x0 -> x6, waiting for transfers between devices: none -> 32.4 us  [the longest x4 23.7 us: collect(): from_left = lax.ppermute(from_left, axis, right)]
    ppermute x0 -> x6, starting transfers between devices: none -> 6.56 us  [the longest x2 3.45 us: collect(): from_right = lax.ppermute(from_right, axis, left)]
    dynamic_update_slice x0 -> x6, local copies, waits for them, and re-layouts: none -> 5.25 us  [the longest x4 3.8 us: collect(): lax.dynamic_update_slice_in_dim(out, from_left, (index - hop) % peers * s...]
  transfers between devices with their start and end apart: 8 -> 12, of which waited for: 8 -> 12; matrix products, arithmetic and copies ran while one was open for 3% -> 2% of each run, Pallas kernels for 0% -> 0%
where the time goes in v1:
time: 218 us; the launch traced here: 217 us
  waiting for transfers between devices  168 us (77%)
  matrix products  17.2 us (8%)
  between operations  13.5 us (6%)
  local copies, waits for them, and re-layouts  8.32 us (4%)
  starting transfers between devices  6.76 us (3%)
  other arithmetic  2.56 us (1%)
    all_gather x2, waiting for transfers between devices, on_device(): lax.all_gather(xb, 'col', axis=1, tiled=True)  64.8 us
    all_gather x2, waiting for transfers between devices, on_device(): x_panel = lax.all_gather(xb, 'row', axis=0, tiled=True)  53.9 us
    ppermute x4, waiting for transfers between devices, collect(): from_left = lax.ppermute(from_left, axis, right)  23.7 us
    all_gather x2, waiting for transfers between devices, on_device(): lax.all_gather(qb, 'col', axis=1, tiled=True)  15.9 us
    ppermute x2, waiting for transfers between devices, collect(): from_right = lax.ppermute(from_right, axis, left)  8.66 us
    dot_general x2, matrix products, on_device(): jnp.dot(lax.all_gather(xb, 'col', axis=1, tiled=True), x_panel, preferred...  6.73 us
    dot_general x2, matrix products, on_device(): jnp.dot(lax.all_gather(xb, 'col', axis=1, tiled=True), q_panel, preferred...  5.38 us
    dot_general x2, matrix products, on_device(): jnp.dot(lax.all_gather(qb, 'col', axis=1, tiled=True), x_panel, preferred...  5.13 us
  transfers between devices with their start and end apart: 12, of which 12 were waited for; matrix products, arithmetic and copies ran while one was open for 2% of the time, Pallas kernels for 0%

profile of v1, /device:TPU:0, one launch (start us, length us, event | category | flops | bytes accessed | tf_op | source)
XLA Modules:
  0.0 216.6 jit_solution(2652369269332553832)
XLA Ops:
  6.5 0.0 all-gather.9.cloned.1.call-start
  6.5 0.8 copy.3
  7.3 0.8 fusion.7
  8.1 0.2 mul.69
  8.3 1.8 fusion.5
  10.1 0.0 all-gather.9.cloned.1.call-update
  10.1 0.0 all-gather.7.cloned.1.call-start
  10.2 0.7 all-gather.7.cloned.1.call-update
  10.9 0.0 all-gather.11.cloned.1.call-start
  10.9 28.7 %all-gather.9.cloned.1.call-done = bf16[2048,256]{1,0:T(8,128)(2,1)} async-done(((bf16[512,256]{1,0:T(8,128)(2,1)}), bf16[2048,256]{1,0:T(8,128)(2,1)}) %all-gather.9.cloned.1.call-update) | async-done | bytes 1048592 | tf_op jit(solution)/shard_map/all_gather | solution.py:57
  39.6 32.5 %all-gather.7.cloned.1.call-done = bf16[512,2048]{1,0:T(8,128)(2,1)} async-done(((bf16[512,256]{1,0:T(8,128)(2,1)}), bf16[512,2048]{1,0:T(8,128)(2,1)}) %all-gather.7.cloned.1.call-update) | async-done | bytes 2097168 | tf_op jit(solution)/shard_map/all_gather | solution.py:59
  72.0 1.0 broadcast.16.clone
  73.1 3.4 %constant_dynamic-update-slice_fusion.7 = (bf16[2048,256]{1,0:T(8,128)(2,1)}, bf16[512,256]{1,0:T(8,128)(2,1)}, f32[512,256]{1,0:T(8,128)S(1)}) fusion(bf16[2048,256]{1,0:T(8,128)(2,1)} %broadcast.16.clone, s32[]{:T(128)S(6)} %select_n.45, f32[64,8,2,128]{3,2,1,0:T(2,128)S(1)} %bitcast.24, bf16[512,2048]{1,0:T(8,128)(2,1)} %all-gather.7.cloned.1.call-done, ...), kind=kOutput, calls=%fused_computation.22 | convolution fusion | flops 537133056 | bytes 4718596 | tf_op jit(solution)/shard_map/dot_general | solution.py:58
  76.4 0.0 all-gather.11.cloned.1.call-update
  76.5 0.0 all-gather.15.cloned.1.call-start
  76.5 1.3 collective-permute-start
  77.8 1.7 collective-permute-start.1
  79.5 7.3 %collective-permute-done = bf16[512,256]{1,0:T(8,128)(2,1)S(1)} collective-permute-done((bf16[512,256]{1,0:T(8,128)(2,1)}, bf16[512,256]{1,0:T(8,128)(2,1)S(1)}, u32[]{:S(2)}, u32[]{:S(2)}) %collective-permute-start) | collective-permute-done | bytes 262176 | tf_op jit(solution)/shard_map/ppermute | solution.py:19
  86.8 0.3 collective-permute-start.2
  87.1 0.7 constant_dynamic-update-slice_fusion.6
  87.8 4.3 %collective-permute-done.1 = bf16[512,256]{1,0:T(8,128)(2,1)S(1)} collective-permute-done((bf16[512,256]{1,0:T(8,128)(2,1)}, bf16[512,256]{1,0:T(8,128)(2,1)S(1)}, u32[]{:S(2)}, u32[]{:S(2)}) %collective-permute-start.1) | collective-permute-done | bytes 262176 | tf_op jit(solution)/shard_map/ppermute | solution.py:24
  92.2 0.7 constant_dynamic-update-slice_fusion.5
  92.9 0.0 copy-start.1
  92.9 4.6 %collective-permute-done.2 = bf16[512,256]{1,0:T(8,128)(2,1)} collective-permute-done((bf16[512,256]{1,0:T(8,128)(2,1)S(1)}, bf16[512,256]{1,0:T(8,128)(2,1)}, u32[]{:S(2)}, u32[]{:S(2)}) %collective-permute-start.2) | collective-permute-done | bytes 262176 | tf_op jit(solution)/shard_map/ppermute | solution.py:19
  97.5 1.7 constant_dynamic-update-slice_fusion.4
  99.1 7.4 %all-gather.11.cloned.1.call-done = bf16[512,2048]{1,0:T(8,128)(2,1)} async-done(((bf16[512,256]{1,0:T(8,128)(2,1)}), bf16[512,2048]{1,0:T(8,128)(2,1)}) %all-gather.11.cloned.1.call-update) | async-done | bytes 2097168 | tf_op jit(solution)/shard_map/all_gather | solution.py:67
  106.5 2.6 %fusion.8 = f32[512,256]{1,0:T(8,128)S(1)} fusion(bf16[512,2048]{1,0:T(8,128)(2,1)} %all-gather.11.cloned.1.call-done, bf16[2048,256]{1,0:T(8,128)(2,1)} %all-gather.9.cloned.1.call-done), kind=kOutput, calls=%fused_computation.23 | convolution fusion | flops 536870912 | bytes 3670016 | tf_op jit(solution)/shard_map/dot_general | solution.py:66
  109.1 0.0 copy-done.1
  109.1 2.6 %fusion.4 = bf16[512,256]{1,0:T(8,128)(2,1)} fusion(f32[512,256]{1,0:T(8,128)S(1)} %fusion.8, bf16[512,2048]{1,0:T(8,128)(2,1)S(1)} %copy-done.1, bf16[2048,256]{1,0:T(8,128)(2,1)} %constant_dynamic-update-slice_fusion.4, f32[512,256]{1,0:T(8,128)S(1)} %get-tuple-element.9, f32[64,8,2,128]{3,2,1,0:T(2,128)S(1)} %bitcast.25), kind=kOutput, calls=%fused_computation.8 | convolution fusion | flops 537526272 | bytes 4980736 | tf_op jit(solution)/shard_map/dot_general | solution.py:71
  111.8 0.0 all-gather.15.cloned.1.call-update
  111.8 0.0 all-gather.13.cloned.1.call-start
  111.8 0.5 all-gather.13.cloned.1.call-update
  112.4 0.0 all-gather.17.cloned.1.call-start
  112.4 25.2 %all-gather.15.cloned.1.call-done = bf16[2048,256]{1,0:T(8,128)(2,1)} async-done(((bf16[512,256]{1,0:T(8,128)(2,1)}), bf16[2048,256]{1,0:T(8,128)(2,1)}) %all-gather.15.cloned.1.call-update) | async-done | bytes 1048592 | tf_op jit(solution)/shard_map/all_gather | solution.py:57
  137.6 32.3 %all-gather.13.cloned.1.call-done = bf16[512,2048]{1,0:T(8,128)(2,1)} async-done(((bf16[512,256]{1,0:T(8,128)(2,1)}), bf16[512,2048]{1,0:T(8,128)(2,1)}) %all-gather.13.cloned.1.call-update) | async-done | bytes 2097168 | tf_op jit(solution)/shard_map/all_gather | solution.py:59
  169.9 1.0 broadcast.16
  171.0 3.4 %constant_dynamic-update-slice_fusion.3 = (bf16[2048,256]{1,0:T(8,128)(2,1)}, bf16[512,256]{1,0:T(8,128)(2,1)}, f32[512,256]{1,0:T(8,128)S(1)}) fusion(bf16[2048,256]{1,0:T(8,128)(2,1)} %broadcast.16, s32[]{:T(128)S(6)} %select_n.45, f32[64,8,2,128]{3,2,1,0:T(2,128)S(1)} %bitcast.26, bf16[512,2048]{1,0:T(8,128)(2,1)} %all-gather.13.cloned.1.call-done, ...), kind=kOutput, calls=%fused_computation.18 | convolution fusion | flops 537133056 | bytes 4718596 | tf_op jit(solution)/shard_map/dot_general | solution.py:58
  174.4 0.0 all-gather.17.cloned.1.call-update
  174.4 1.3 collective-permute-start.3
  175.6 1.7 collective-permute-start.4
  177.4 7.3 %collective-permute-done.3 = bf16[512,256]{1,0:T(8,128)(2,1)S(1)} collective-permute-done((bf16[512,256]{1,0:T(8,128)(2,1)}, bf16[512,256]{1,0:T(8,128)(2,1)S(1)}, u32[]{:S(2)}, u32[]{:S(2)}) %collective-permute-start.3) | collective-permute-done | bytes 262176 | tf_op jit(solution)/shard_map/ppermute | solution.py:19
  184.7 0.3 collective-permute-start.5
  185.0 0.7 constant_dynamic-update-slice_fusion.2
  185.7 4.3 %collective-permute-done.4 = bf16[512,256]{1,0:T(8,128)(2,1)S(1)} collective-permute-done((bf16[512,256]{1,0:T(8,128)(2,1)}, bf16[512,256]{1,0:T(8,128)(2,1)S(1)}, u32[]{:S(2)}, u32[]{:S(2)}) %collective-permute-start.4) | collective-permute-done | bytes 262176 | tf_op jit(solution)/shard_map/ppermute | solution.py:24
  190.0 0.7 constant_dynamic-update-slice_fusion.1
  190.7 0.0 copy-start
  190.8 4.5 %collective-permute-done.5 = bf16[512,256]{1,0:T(8,128)(2,1)S(1)} collective-permute-done((bf16[512,256]{1,0:T(8,128)(2,1)S(1)}, bf16[512,256]{1,0:T(8,128)(2,1)S(1)}, u32[]{:S(2)}, u32[]{:S(2)}) %collective-permute-start.5) | collective-permute-done | bytes 262176 | tf_op jit(solution)/shard_map/ppermute | solution.py:19
  195.2 0.7 constant_dynamic-update-slice_fusion
  195.9 8.5 %all-gather.17.cloned.1.call-done = bf16[512,2048]{1,0:T(8,128)(2,1)} async-done(((bf16[512,256]{1,0:T(8,128)(2,1)}), bf16[512,2048]{1,0:T(8,128)(2,1)}) %all-gather.17.cloned.1.call-update) | async-done | bytes 2097168 | tf_op jit(solution)/shard_map/all_gather | solution.py:67
  204.4 2.6 %fusion.9 = f32[512,256]{1,0:T(8,128)S(1)} fusion(bf16[512,2048]{1,0:T(8,128)(2,1)} %all-gather.17.cloned.1.call-done, bf16[2048,256]{1,0:T(8,128)(2,1)} %all-gather.15.cloned.1.call-done), kind=kOutput, calls=%fused_computation.24 | convolution fusion | flops 536870912 | bytes 3670016 | tf_op jit(solution)/shard_map/dot_general | solution.py:66
  207.0 0.0 copy-done
  207.0 2.7 %fusion.3 = f32[512,256]{1,0:T(8,128)} fusion(f32[512,256]{1,0:T(8,128)S(1)} %fusion.9, bf16[512,2048]{1,0:T(8,128)(2,1)S(1)} %copy-done, bf16[2048,256]{1,0:T(8,128)(2,1)} %constant_dynamic-update-slice_fusion, f32[512,256]{1,0:T(8,128)S(1)} %get-tuple-element.10, f32[64,8,2,128]{3,2,1,0:T(2,128)S(1)} %bitcast.27), kind=kOutput, calls=%fused_computation.7 | convolution fusion | flops 537395200 | bytes 5242880 | tf_op jit(solution)/shard_map/dot_general | solution.py:71
Async XLA Ops:
  6.5 33.0 %all-gather.9.cloned.1.call-start = ((), (), s32[]{:S(2)}) async-start(), calls=%async_computation.1 | async-start | bytes 1310720 | tf_op jit(solution)/shard_map/all_gather | solution.py:57
  10.1 61.9 %all-gather.7.cloned.1.call-start = ((), (), s32[]{:S(2)}) async-start(), calls=%async_computation | async-start | bytes 2359296 | tf_op jit(solution)/shard_map/all_gather | solution.py:59
  10.9 95.7 %all-gather.11.cloned.1.call-start = ((), (), s32[]{:S(2)}) async-start(), calls=%async_computation.2 | async-start | bytes 2359296 | tf_op jit(solution)/shard_map/all_gather | solution.py:67
  76.5 61.2 %all-gather.15.cloned.1.call-start = ((), (), s32[]{:S(2)}) async-start(), calls=%async_computation.4 | async-start | bytes 1310720 | tf_op jit(solution)/shard_map/all_gather | solution.py:57
  76.5 10.3 %collective-permute-start = (bf16[512,256]{1,0:T(8,128)(2,1)}, bf16[512,256]{1,0:T(8,128)(2,1)S(1)}, u32[]{:S(2)}, u32[]{:S(2)}) collective-permute-start(bf16[512,256]{1,0:T(8,128)(2,1)} %get-tuple-element.8), channel_id=1, source_target_pairs={{0,8},{8,16},{16,24},{24,0},{1,9},{9,17},{17,25},{25,1},{2,10},{10... | collective-permute-start | bytes 786440 | tf_op jit(solution)/shard_map/ppermute | solution.py:19
  77.8 14.4 %collective-permute-start.1 = (bf16[512,256]{1,0:T(8,128)(2,1)}, bf16[512,256]{1,0:T(8,128)(2,1)S(1)}, u32[]{:S(2)}, u32[]{:S(2)}) collective-permute-start(bf16[512,256]{1,0:T(8,128)(2,1)} %get-tuple-element.8), channel_id=1, source_target_pairs={{0,24},{8,0},{16,8},{24,16},{1,25},{9,1},{17,9},{25,17},{2,26},{10... | collective-permute-start | bytes 786440 | tf_op jit(solution)/shard_map/ppermute | solution.py:24
  86.8 10.7 %collective-permute-start.2 = (bf16[512,256]{1,0:T(8,128)(2,1)S(1)}, bf16[512,256]{1,0:T(8,128)(2,1)}, u32[]{:S(2)}, u32[]{:S(2)}) collective-permute-start(bf16[512,256]{1,0:T(8,128)(2,1)S(1)} %collective-permute-done), channel_id=1, source_target_pairs={{0,8},{8,16},{16,24},{24,0},{1,9},{9,17},{17,25},{25,1},{2,10},{10... | collective-permute-start | bytes 786440 | tf_op jit(solution)/shard_map/ppermute | solution.py:19
  92.9 16.2 %copy-start.1 = (bf16[512,2048]{1,0:T(8,128)(2,1)S(1)}, bf16[512,2048]{1,0:T(8,128)(2,1)}, u32[]{:S(2)}) copy-start(bf16[512,2048]{1,0:T(8,128)(2,1)} %all-gather.7.cloned.1.call-done) | copy-start | bytes 6291460
  111.8 58.2 %all-gather.13.cloned.1.call-start = ((), (), s32[]{:S(2)}) async-start(), calls=%async_computation.3 | async-start | bytes 2359296 | tf_op jit(solution)/shard_map/all_gather | solution.py:59
  112.4 92.1 %all-gather.17.cloned.1.call-start = ((), (), s32[]{:S(2)}) async-start(), calls=%async_computation.5 | async-start | bytes 2359296 | tf_op jit(solution)/shard_map/all_gather | solution.py:67
  174.4 10.3 %collective-permute-start.3 = (bf16[512,256]{1,0:T(8,128)(2,1)}, bf16[512,256]{1,0:T(8,128)(2,1)S(1)}, u32[]{:S(2)}, u32[]{:S(2)}) collective-permute-start(bf16[512,256]{1,0:T(8,128)(2,1)} %get-tuple-element.6), channel_id=1, source_target_pairs={{0,8},{8,16},{16,24},{24,0},{1,9},{9,17},{17,25},{25,1},{2,10},{10... | collective-permute-start | bytes 786440 | tf_op jit(solution)/shard_map/ppermute | solution.py:19
  175.6 14.4 %collective-permute-start.4 = (bf16[512,256]{1,0:T(8,128)(2,1)}, bf16[512,256]{1,0:T(8,128)(2,1)S(1)}, u32[]{:S(2)}, u32[]{:S(2)}) collective-permute-start(bf16[512,256]{1,0:T(8,128)(2,1)} %get-tuple-element.6), channel_id=1, source_target_pairs={{0,24},{8,0},{16,8},{24,16},{1,25},{9,1},{17,9},{25,17},{2,26},{10... | collective-permute-start | bytes 786440 | tf_op jit(solution)/shard_map/ppermute | solution.py:24
  184.7 10.6 %collective-permute-start.5 = (bf16[512,256]{1,0:T(8,128)(2,1)S(1)}, bf16[512,256]{1,0:T(8,128)(2,1)S(1)}, u32[]{:S(2)}, u32[]{:S(2)}) collective-permute-start(bf16[512,256]{1,0:T(8,128)(2,1)S(1)} %collective-permute-done.3), channel_id=1, source_target_pairs={{0,8},{8,16},{16,24},{24,0},{1,9},{9,17},{17,25},{25,1},{2,10},{10... | collective-permute-start | bytes 786440 | tf_op jit(solution)/shard_map/ppermute | solution.py:19
  190.7 16.3 %copy-start = (bf16[512,2048]{1,0:T(8,128)(2,1)S(1)}, bf16[512,2048]{1,0:T(8,128)(2,1)}, u32[]{:S(2)}) copy-start(bf16[512,2048]{1,0:T(8,128)(2,1)} %all-gather.13.cloned.1.call-done) | copy-start | bytes 6291460
Sparse Core Ops, SparseCore 0:
  10.2 29.3 all-gather.8
  41.2 30.8 all-gather.6
  76.6 29.8 all-gather.10
  111.9 25.6 all-gather.14
  139.1 30.8 all-gather.12
  174.5 29.8 all-gather.16
